TPU v7x, 256 devices: a whole 4x4x8 slice. The times are simulated.
256 devices in a mesh: seq: 16 (over x, y), exp: 16 (over z, core).
Axes of the slice: x: 4, y: 4, z: 8, core: 2. Of those that a mesh axis runs over, the one named last changes fastest.
Arguments:
- tokens: bfloat16 [16384, 2048], P('seq', 'exp'), may hold values from -51 to 51
- in_gain: float32 [2048], replicated, may hold values from 0.1 to 1.9
- w_query: bfloat16 [2048, 2048], P(None, 'exp'), may hold values from -0.125 to 0.125
- w_key: bfloat16 [2048, 2048], P(None, 'exp'), may hold values from -0.125 to 0.125
- w_value: bfloat16 [2048, 4096], P(None, 'exp'), may hold values from -0.125 to 0.125
- w_zgate: bfloat16 [2048, 4096], P(None, 'exp'), may hold values from -0.125 to 0.125
- conv_query: float32 [4, 2048], P(None, 'exp'), may hold values from -3 to 3
- conv_key: float32 [4, 2048], P(None, 'exp'), may hold values from -3 to 3
- conv_value: float32 [4, 4096], P(None, 'exp'), may hold values from -3 to 3
- log_decay: float32 [16384, 32], P('seq', 'exp'), may hold values from -1.7 to 0
- write_rate: float32 [16384, 32], P('seq', 'exp'), may hold values from 0 to 1
- norm_gain: float32 [128], replicated, may hold values from 0.1 to 1.9
- w_out: bfloat16 [4096, 2048], P('exp'), may hold values from -0.09375 to 0.09375
- post_gain: float32 [2048], replicated, may hold values from 0.1 to 1.9
- expert_ids: int32 [16384, 2], P(('seq', 'exp')), may hold values from 0 to 15, as said below
- route_weight: float32 [16384, 2], P(('seq', 'exp')), may hold values from 0.1 to 1
- w_gate: bfloat16 [16, 2048, 512], P('exp'), may hold values from -0.125 to 0.125
- w_up: bfloat16 [16, 2048, 512], P('exp'), may hold values from -0.125 to 0.125
- w_down: bfloat16 [16, 512, 2048], P('exp'), may hold values from -0.25 to 0.25
Outputs:
- block_out: bfloat16 [16384, 2048], P(('seq', 'exp'))
Inputs may be any that keep to these rules, and one draw needn't show every extreme that they name: `expert_ids`: each row names 2 different experts. In each aligned block of 64 rows (the rows of one device) no expert is named more than 16 times, and in every aligned block of 1024 rows some expert is named exactly 16 times in each of its blocks of 64 rows.
All inputs are finite; a program needn't handle non-finite values.
Results may differ from a plain program's by a relative error of at most 0.015.
Values may be sent and summed in bfloat16 or wider, within the bound.
No kernel may reach another device: no remote copies, remote signals or barrier semaphores. Data moves between devices by JAX's collectives and lax.ppermute only.
A program may use at most 128 MiB of HBM per device.

v0:
```python
import jax
import jax.numpy as jnp
from jax import lax
from jax.sharding import PartitionSpec as P

DK = 128
DV = 128
STRETCH = 64
EPS = 1e-06
HIGH = lax.Precision.HIGHEST


def passed_along(block, axis, distance):
    devices = range(lax.axis_size(axis))
    route = [(i - distance, i) for i in devices if i - distance in devices]
    return lax.ppermute(block, axis, route)


def rms_scale(values, gain):
    return values * lax.rsqrt(jnp.mean(values * values, -1, keepdims=True) + EPS) * gain


def mix(form, left_arr, right_arr):
    return jnp.einsum(form, left_arr, right_arr, precision=HIGH)


def unit_heads(values, heads):
    shaped = values.reshape(values.shape[0], heads, -1)
    return shaped * lax.rsqrt(jnp.sum(shaped * shaped, -1, keepdims=True) + EPS)


def per_device(
    tokens,
    in_gain,
    w_query,
    w_key,
    w_value,
    w_zgate,
    conv_query,
    conv_key,
    conv_value,
    log_decay,
    write_rate,
    norm_gain,
    w_out,
    post_gain,
    expert_ids,
    route_weight,
    w_gate,
    w_up,
    w_down,
):
    whole = lax.all_gather(tokens, "exp", axis=1, tiled=True)
    x_float = whole.astype(jnp.float32)
    normed = rms_scale(x_float, in_gain).astype(jnp.bfloat16)

    def project(weight):
        return jnp.dot(normed, weight, preferred_element_type=jnp.float32).astype(jnp.bfloat16)

    projected = jnp.concatenate([project(w_query), project(w_key), project(w_value)], 1)
    z_gate = project(w_zgate)
    conv_all = jnp.concatenate([conv_query, conv_key, conv_value], 1)
    taps = conv_all.shape[0]
    length = projected.shape[0]
    tail = projected[length - (taps - 1) :]
    before = passed_along(tail, "seq", 1)
    extended = jnp.concatenate([before, projected], 0).astype(jnp.float32)
    conv_out = conv_all[0] * extended[0:length]
    for index in range(1, taps):
        conv_out = conv_out + conv_all[index] * extended[index : index + length]
    conv_out = jax.nn.silu(conv_out)
    width_q = w_query.shape[1]
    width_k = w_key.shape[1]
    key_heads = width_q // DK
    value_heads = w_value.shape[1] // DV
    group = value_heads // key_heads
    query = unit_heads(conv_out[:, :width_q], key_heads) * DK ** (-0.5)
    keyvec = unit_heads(conv_out[:, width_q : width_q + width_k], key_heads)
    values = conv_out[:, width_q + width_k :].reshape(length, value_heads, DV)
    query = jnp.repeat(query, group, axis=1)
    keyvec = jnp.repeat(keyvec, group, axis=1)
    blocks = length // STRETCH

    def by_block(array):
        return array.reshape(blocks, STRETCH, value_heads, -1).transpose(2, 0, 1, 3)

    q_blk = by_block(query)
    k_blk = by_block(keyvec)
    v_blk = by_block(values)
    g_blk = log_decay.reshape(blocks, STRETCH, value_heads).transpose(2, 0, 1)
    b_blk = write_rate.reshape(blocks, STRETCH, value_heads).transpose(2, 0, 1)
    cumul = jnp.cumsum(g_blk, -1)
    last_cum = cumul[..., -1:]
    places = jnp.arange(STRETCH)
    lower_incl = places[:, None] >= places[None, :]
    lower_strict = places[:, None] > places[None, :]
    spread_log = cumul[..., :, None] - cumul[..., None, :]
    ratio_incl = jnp.where(lower_incl, jnp.exp(jnp.where(lower_incl, spread_log, 0.0)), 0.0)
    key_gram = mix("hnid,hnjd->hnij", k_blk, k_blk)
    system = jnp.eye(STRETCH, dtype=jnp.float32) + jnp.where(
        lower_strict, b_blk[..., None] * key_gram * ratio_incl, 0.0
    )
    decay_in = jnp.exp(cumul)[..., None]
    right_side = jnp.concatenate(
        [b_blk[..., None] * decay_in * k_blk, b_blk[..., None] * v_blk], -1
    )
    solved = jax.scipy.linalg.solve_triangular(system, right_side, lower=True, unit_diagonal=True)
    w_mat = solved[..., :DK]
    u_mat = solved[..., DK:]
    key_tail = k_blk * jnp.exp(last_cum - cumul)[..., None]
    eye_key = jnp.eye(DK, dtype=jnp.float32)
    transit = jnp.exp(last_cum)[..., None] * eye_key - mix("hnik,hnil->hnkl", w_mat, key_tail)
    inject = mix("hniv,hnik->hnvk", u_mat, key_tail)

    def local_step(carry, pair):
        map_pre, add_pre = carry
        map_now, add_now = pair
        new_carry = (
            mix("hkl,hlm->hkm", map_pre, map_now),
            mix("hvl,hlm->hvm", add_pre, map_now) + add_now,
        )
        return (new_carry, carry)

    ident_maps = jnp.broadcast_to(eye_key, (value_heads, DK, DK))
    zero_add = jnp.zeros((value_heads, DV, DK), jnp.float32)
    (map_total, add_total), (map_prefix, add_prefix) = lax.scan(
        local_step,
        (ident_maps, zero_add),
        (transit.transpose(1, 0, 2, 3), inject.transpose(1, 0, 2, 3)),
    )

    def relay(step_index, state):
        passed = mix("hvk,hkl->hvl", state, map_total) + add_total
        return passed_along(passed.astype(jnp.bfloat16), "seq", 1).astype(passed.dtype)

    incoming = lax.fori_loop(0, lax.axis_size("seq") - 1, relay, zero_add)
    starts = (mix("hvk,nhkl->nhvl", incoming, map_prefix) + add_prefix).transpose(1, 0, 2, 3)
    new_values = u_mat - mix("hnik,hnvk->hniv", w_mat, starts)
    scores = mix("hnid,hnjd->hnij", q_blk, k_blk) * ratio_incl
    out_blk = decay_in * mix("hnik,hnvk->hniv", q_blk, starts) + mix(
        "hnij,hnjv->hniv", scores, new_values
    )
    delta_out = out_blk.transpose(1, 2, 0, 3).reshape(length, value_heads, DV)
    gate_z = z_gate.astype(jnp.float32).reshape(length, value_heads, DV)
    gated = (
        (rms_scale(delta_out, norm_gain) * jax.nn.silu(gate_z))
        .astype(jnp.bfloat16)
        .reshape(length, value_heads * DV)
    )
    n_exp = lax.axis_size("exp")
    row_share = length // n_exp
    attn_rows = lax.psum_scatter(
        jnp.dot(gated, w_out, preferred_element_type=jnp.float32).astype(jnp.bfloat16),
        "exp",
        scatter_dimension=0,
        tiled=True,
    ).astype(jnp.float32)
    own_rows = lax.dynamic_slice_in_dim(
        whole, lax.axis_index("exp") * row_share, row_share, 0
    ).astype(jnp.float32)
    resid = own_rows + attn_rows
    post = rms_scale(resid, post_gain).astype(jnp.bfloat16)
    topk = expert_ids.shape[1]
    experts = w_gate.shape[0] * n_exp
    capacity = 2 * row_share * topk // experts
    flat_ids = expert_ids.reshape(-1)
    hits = (flat_ids[:, None] == jnp.arange(experts)[None, :]).astype(jnp.int32)
    earlier_hits = jnp.cumsum(hits, 0) - hits
    slot_of = jnp.sum(earlier_hits * hits, 1)
    target = flat_ids * capacity + slot_of
    route_map = (target[:, None] == jnp.arange(experts * capacity)[None, :]).astype(jnp.bfloat16)
    spread_rows = jnp.repeat(post, topk, axis=0)
    outgoing = jnp.einsum(
        "rp,rd->pd", route_map, spread_rows, preferred_element_type=jnp.float32
    ).astype(jnp.bfloat16)
    outgoing = outgoing.reshape(experts, 1, capacity, post.shape[1])
    batch = lax.all_to_all(outgoing, "exp", split_axis=0, concat_axis=1, tiled=True)
    gate_v = jnp.einsum("esnd,edf->esnf", batch, w_gate, preferred_element_type=jnp.float32)
    up_v = jnp.einsum("esnd,edf->esnf", batch, w_up, preferred_element_type=jnp.float32)
    act = (jax.nn.silu(gate_v) * up_v).astype(jnp.bfloat16)
    processed = jnp.einsum(
        "esnf,efd->esnd", act, w_down, preferred_element_type=jnp.float32
    ).astype(jnp.bfloat16)
    returned = lax.all_to_all(processed, "exp", split_axis=1, concat_axis=0, tiled=True)
    flat_back = returned.reshape(experts * capacity, post.shape[1])
    fetched = jnp.dot(route_map, flat_back, preferred_element_type=jnp.float32).reshape(
        row_share, topk, post.shape[1]
    )
    moe_sum = jnp.sum(route_weight[..., None] * fetched, 1)
    return (resid + moe_sum).astype(jnp.bfloat16)


def solution(mesh):
    return jax.shard_map(
        per_device,
        mesh=mesh,
        in_specs=(
            P("seq", "exp"),
            P(),
            P(None, "exp"),
            P(None, "exp"),
            P(None, "exp"),
            P(None, "exp"),
            P(None, "exp"),
            P(None, "exp"),
            P(None, "exp"),
            P("seq", "exp"),
            P("seq", "exp"),
            P(),
            P("exp", None),
            P(),
            P(("seq", "exp"), None),
            P(("seq", "exp"), None),
            P("exp", None, None),
            P("exp", None, None),
            P("exp", None, None),
        ),
        out_specs=P(("seq", "exp"), None),
        check_vma=False,
    )
```

profile of v0, /device:TPU:1, one launch (start us, length us, event | category | flops | bytes accessed | tf_op | source)
XLA Modules:
  0.0 643.8 jit_solution(5141278856322808113)
XLA Ops:
  15.9 46.7 %all-gather.2.cloned.1.call-done = bf16[1024,2048]{1,0:T(8,128)(2,1)} async-done(((bf16[1024,128]{1,0:T(8,128)(2,1)}), bf16[1024,2048]{1,0:T(8,128)(2,1)}) %all-gather.2.cloned.1.call-update) | async-done | bytes 4194320 | tf_op jit(solution)/shard_map/all_gather | solution.py:53
  72.5 3.4 collective-permute-start.1
  84.2 3.7 fusion.53
  88.0 158.7 %custom-call.4 = f32[2,16,1,64,64]{3,4,2,1,0:T(8,128)} custom-call(f32[2,16,1,64,64]{4,3,2,1,0:T(8,128)} %fusion.53), custom_call_target="InvertDiagBlocksLowerTriangular" | custom-call | tf_op jit(solution)/shard_map/jit(_solve_triangular)/vmap(vmap())/triangular_solve | solution.py:107
  248.0 3.3 reshape.217
  251.3 3.3 copy.88
  258.5 5.1 convolution_bitcast_fusion.2
  263.7 5.4 bitcast_subtract_fusion
  269.1 70.9 %while.28 = (s32[]{:T(128)}, f32[2,128,128]{1,2,0:T(8,128)S(1)}, f32[2,128,128]{1,2,0:T(8,128)S(1)}, f32[16,2,128,128]{2,3,0,1:T(8,128)}, f32[16,2,128,128]{2,3,...) while((s32[]{:T(128)}, f32[2,128,128]{1,2,0:T(8,128)S(1)}, ...), condition=%wide.region_5.6_spmd.clone, body=%wide.region_4.5_spmd.clone.sunk | while | flops 100761600 | bytes 2492012 | solution.py:126
  340.2 104.4 %while.29 = (s32[]{:T(128)}, f32[2,128,128]{2,1,0:T(8,128)S(1)}, f32[2,128,128]{2,1,0:T(8,128)S(1)}, f32[2,128,128]{2,1,0:T(8,128)S(1)}, s32[]{:T(128)}, /*index=5*/s32[]{:T(128)}) while((s32[]{:T(128)}, f32[2,128,128]{2,1,0:T(8,128)S(1)}, f32[2,128,128]{2,1,0:T(8,128)S(1)}, f32[2,128,128]{2,1,0:T(8,128)S(1)}, s32[]{:T(128)}, ...), condition=%wide.region_7.8_spmd.clone, body=%wide.region_6.7_spmd.clone.sunk | while | flops 50462720 | bytes 917623 | solution.py:136
  340.6 4.1 collective-permute-start
  346.4 3.7 collective-permute-start
  351.7 3.7 collective-permute-start
  357.0 3.7 collective-permute-start
  362.3 5.8 collective-permute-start
  369.8 5.8 collective-permute-start
  377.2 5.8 collective-permute-start
  384.6 5.8 collective-permute-start
  392.5 5.7 collective-permute-start
  399.8 6.1 collective-permute-start
  407.5 6.0 collective-permute-start
  415.2 5.8 collective-permute-start
  422.6 5.8 collective-permute-start
  430.0 5.8 collective-permute-start
  437.5 5.8 collective-permute-start
  444.6 4.3 bitcast_add_fusion
  463.2 9.4 %convolution_convert_fusion = bf16[1024,2048]{1,0:T(8,128)(2,1)} fusion(bf16[256,2048]{1,0:T(8,128)(2,1)} %param.35, bf16[1024,2048]{1,0:T(8,128)(2,1)} %copy-done.1, bf16[2048,256]{1,0:T(8,128)(2,1)} %param.28, f32[128,8,2,128]{3,2,1,0:T(2,128)S(1)} %bitcast.176, f32[128,8,2,128]{3,2,1,0:T(2,128)} %bitcast.177, f32[256]{0:T(256)S(1)} %copy-done.31), kind=kOutput, calls=%fused_computation.27 | convolution fusion | flops 2152202240 | bytes 12583936 | tf_op jit(solution)/shard_map/dot_general | solution.py:153
  474.1 84.1 %reduce-scatter.2.cloned.1.call-done = bf16[64,2048]{1,0:T(8,128)(2,1)} async-done(((bf16[1024,2048]{1,0:T(8,128)(2,1)}), bf16[64,2048]{1,0:T(8,128)(2,1)}) %reduce-scatter.2.cloned.1.call-update) | async-done | bytes 262160 | tf_op jit(solution)/shard_map/reduce_scatter | solution.py:152
  561.7 36.3 %all_to_all.8 = bf16[16,1,16,2048]{3,2,1,0:T(8,128)(2,1)S(1)} all-to-all(bf16[16,1,16,2048]{3,2,1,0:T(8,128)(2,1)S(1)} %bitcast.174), channel_id=1, replica_groups=mesh['seq'=16,'exp'=16] {'exp'}, dimensions={0} | all-to-all | bytes 2097152 | tf_op jit(solution)/shard_map/all_to_all | solution.py:177
  599.5 4.0 fusion.19
  603.5 3.7 all-to-all-start.1
  607.4 27.1 %all-to-all-done.1 = bf16[1,16,16,2048]{3,2,0,1:T(8,128)(2,1)S(1)} async-done(((bf16[1,16,16,2048]{3,2,0,1:T(8,128)(2,1)}), bf16[1,16,16,2048]{3,2,0,1:T(8,128)(2,1)S(1)}, u32[]{:S(2)}, u32[]{:S(2)}) %all-to-all-start.1) | async-done | bytes 1048608 | tf_op jit(solution)/shard_map/all_to_all | solution.py:184
  (293 shorter events, 149.8 us)
Async XLA Ops:
  6.5 593.0 %copy-start = (bf16[1,512,2048]{2,1,0:T(8,128)(2,1)S(1)}, bf16[1,512,2048]{2,1,0:T(8,128)(2,1)}, u32[]{:S(2)}) copy-start(bf16[1,512,2048]{2,1,0:T(8,128)(2,1)} %param.41) | copy-start | bytes 6291460
  6.5 56.1 %all-gather.2.cloned.1.call-start = ((), (), s32[]{:S(2)}) async-start(), calls=%async_computation.3 | async-start | bytes 4456448 | tf_op jit(solution)/shard_map/all_gather | solution.py:53
  7.3 550.9 %reduce-scatter.2.cloned.1.call-start = ((), (), s32[]{:S(2)}) async-start(), calls=%async_computation.4 | async-start | bytes 4456448 | tf_op jit(solution)/shard_map/reduce_scatter | solution.py:152
  8.9 57.0 %copy-start.15 = (f32[16,64,2]{1,0,2:T(8,128)}, f32[16,64,2]{1,0,2:T(8,128)S(1)}, u32[]{:S(2)}) copy-start(f32[16,64,2]{1,0,2:T(8,128)S(1)} %reshape.203) | copy-start | bytes 24580
  15.9 49.9 %copy-start.20 = (f32[2048]{0:T(1024)S(1)}, f32[2048]{0:T(1024)}, u32[]{:S(2)}) copy-start(f32[2048]{0:T(1024)} %param.24) | copy-start | bytes 24580
  72.5 5.7 collective-permute-start.1
  84.2 162.4 %copy-start.18 = (f32[2,16,64]{2,1,0:T(8,128)S(1)}, f32[2,16,64]{2,1,0:T(8,128)}, u32[]{:S(2)}) copy-start(f32[2,16,64]{2,1,0:T(8,128)} %get-tuple-element.187) | copy-start | bytes 24580
  258.5 10.6 %copy-start.5 = (f32[2,16,64,256]{3,2,1,0:T(8,128)}, f32[2,16,64,256]{3,2,1,0:T(8,128)S(1)}, u32[]{:S(2)}) copy-start(f32[2,16,64,256]{3,2,1,0:T(8,128)S(1)} %fusion.23) | copy-start | bytes 6291460
  258.5 5.2 copy-start.27
  340.6 5.4 collective-permute-start
  346.4 5.0 collective-permute-start
  351.7 5.0 collective-permute-start
  357.0 5.0 collective-permute-start
  362.3 7.1 %collective-permute-start = (bf16[2,128,128]{2,1,0:T(8,128)(2,1)S(1)}, bf16[2,128,128]{2,1,0:T(8,128)(2,1)S(1)}, u32[]{:S(2)}, u32[]{:S(2)}) collective-permute-start(bf16[2,128,128]{2,1,0:T(8,128)(2,1)S(1)} %fusion.141), channel_id=1, source_target_pairs={{0,16},{16,32},{32,48},{48,64},{64,80},{80,96},{96,112},{112,128},... | collective-permute-start | bytes 196616 | tf_op jit(solution)/shard_map/while/body/eval_jaxpr/ppermute | solution.py:16
  369.8 7.1 %collective-permute-start = (bf16[2,128,128]{2,1,0:T(8,128)(2,1)S(1)}, bf16[2,128,128]{2,1,0:T(8,128)(2,1)S(1)}, u32[]{:S(2)}, u32[]{:S(2)}) collective-permute-start(bf16[2,128,128]{2,1,0:T(8,128)(2,1)S(1)} %fusion.141), channel_id=1, source_target_pairs={{0,16},{16,32},{32,48},{48,64},{64,80},{80,96},{96,112},{112,128},... | collective-permute-start | bytes 196616 | tf_op jit(solution)/shard_map/while/body/eval_jaxpr/ppermute | solution.py:16
  377.2 7.1 %collective-permute-start = (bf16[2,128,128]{2,1,0:T(8,128)(2,1)S(1)}, bf16[2,128,128]{2,1,0:T(8,128)(2,1)S(1)}, u32[]{:S(2)}, u32[]{:S(2)}) collective-permute-start(bf16[2,128,128]{2,1,0:T(8,128)(2,1)S(1)} %fusion.141), channel_id=1, source_target_pairs={{0,16},{16,32},{32,48},{48,64},{64,80},{80,96},{96,112},{112,128},... | collective-permute-start | bytes 196616 | tf_op jit(solution)/shard_map/while/body/eval_jaxpr/ppermute | solution.py:16
  384.6 7.5 %collective-permute-start = (bf16[2,128,128]{2,1,0:T(8,128)(2,1)S(1)}, bf16[2,128,128]{2,1,0:T(8,128)(2,1)S(1)}, u32[]{:S(2)}, u32[]{:S(2)}) collective-permute-start(bf16[2,128,128]{2,1,0:T(8,128)(2,1)S(1)} %fusion.141), channel_id=1, source_target_pairs={{0,16},{16,32},{32,48},{48,64},{64,80},{80,96},{96,112},{112,128},... | collective-permute-start | bytes 196616 | tf_op jit(solution)/shard_map/while/body/eval_jaxpr/ppermute | solution.py:16
  392.5 7.0 %collective-permute-start = (bf16[2,128,128]{2,1,0:T(8,128)(2,1)S(1)}, bf16[2,128,128]{2,1,0:T(8,128)(2,1)S(1)}, u32[]{:S(2)}, u32[]{:S(2)}) collective-permute-start(bf16[2,128,128]{2,1,0:T(8,128)(2,1)S(1)} %fusion.141), channel_id=1, source_target_pairs={{0,16},{16,32},{32,48},{48,64},{64,80},{80,96},{96,112},{112,128},... | collective-permute-start | bytes 196616 | tf_op jit(solution)/shard_map/while/body/eval_jaxpr/ppermute | solution.py:16
  399.8 7.4 %collective-permute-start = (bf16[2,128,128]{2,1,0:T(8,128)(2,1)S(1)}, bf16[2,128,128]{2,1,0:T(8,128)(2,1)S(1)}, u32[]{:S(2)}, u32[]{:S(2)}) collective-permute-start(bf16[2,128,128]{2,1,0:T(8,128)(2,1)S(1)} %fusion.141), channel_id=1, source_target_pairs={{0,16},{16,32},{32,48},{48,64},{64,80},{80,96},{96,112},{112,128},... | collective-permute-start | bytes 196616 | tf_op jit(solution)/shard_map/while/body/eval_jaxpr/ppermute | solution.py:16
  407.5 7.4 %collective-permute-start = (bf16[2,128,128]{2,1,0:T(8,128)(2,1)S(1)}, bf16[2,128,128]{2,1,0:T(8,128)(2,1)S(1)}, u32[]{:S(2)}, u32[]{:S(2)}) collective-permute-start(bf16[2,128,128]{2,1,0:T(8,128)(2,1)S(1)} %fusion.141), channel_id=1, source_target_pairs={{0,16},{16,32},{32,48},{48,64},{64,80},{80,96},{96,112},{112,128},... | collective-permute-start | bytes 196616 | tf_op jit(solution)/shard_map/while/body/eval_jaxpr/ppermute | solution.py:16
  415.2 7.1 %collective-permute-start = (bf16[2,128,128]{2,1,0:T(8,128)(2,1)S(1)}, bf16[2,128,128]{2,1,0:T(8,128)(2,1)S(1)}, u32[]{:S(2)}, u32[]{:S(2)}) collective-permute-start(bf16[2,128,128]{2,1,0:T(8,128)(2,1)S(1)} %fusion.141), channel_id=1, source_target_pairs={{0,16},{16,32},{32,48},{48,64},{64,80},{80,96},{96,112},{112,128},... | collective-permute-start | bytes 196616 | tf_op jit(solution)/shard_map/while/body/eval_jaxpr/ppermute | solution.py:16
  422.6 7.1 %collective-permute-start = (bf16[2,128,128]{2,1,0:T(8,128)(2,1)S(1)}, bf16[2,128,128]{2,1,0:T(8,128)(2,1)S(1)}, u32[]{:S(2)}, u32[]{:S(2)}) collective-permute-start(bf16[2,128,128]{2,1,0:T(8,128)(2,1)S(1)} %fusion.141), channel_id=1, source_target_pairs={{0,16},{16,32},{32,48},{48,64},{64,80},{80,96},{96,112},{112,128},... | collective-permute-start | bytes 196616 | tf_op jit(solution)/shard_map/while/body/eval_jaxpr/ppermute | solution.py:16
  430.0 7.1 %collective-permute-start = (bf16[2,128,128]{2,1,0:T(8,128)(2,1)S(1)}, bf16[2,128,128]{2,1,0:T(8,128)(2,1)S(1)}, u32[]{:S(2)}, u32[]{:S(2)}) collective-permute-start(bf16[2,128,128]{2,1,0:T(8,128)(2,1)S(1)} %fusion.141), channel_id=1, source_target_pairs={{0,16},{16,32},{32,48},{48,64},{64,80},{80,96},{96,112},{112,128},... | collective-permute-start | bytes 196616 | tf_op jit(solution)/shard_map/while/body/eval_jaxpr/ppermute | solution.py:16
  437.5 7.1 %collective-permute-start = (bf16[2,128,128]{2,1,0:T(8,128)(2,1)S(1)}, bf16[2,128,128]{2,1,0:T(8,128)(2,1)S(1)}, u32[]{:S(2)}, u32[]{:S(2)}) collective-permute-start(bf16[2,128,128]{2,1,0:T(8,128)(2,1)S(1)} %fusion.141), channel_id=1, source_target_pairs={{0,16},{16,32},{32,48},{48,64},{64,80},{80,96},{96,112},{112,128},... | collective-permute-start | bytes 196616 | tf_op jit(solution)/shard_map/while/body/eval_jaxpr/ppermute | solution.py:16
  444.6 4.4 copy-start.6
  449.0 4.4 copy-start.19
  458.8 4.4 copy-start.31
  472.7 86.7 %copy-start.21 = (f32[2048]{0:T(1024)S(1)}, f32[2048]{0:T(1024)}, u32[]{:S(2)}) copy-start(f32[2048]{0:T(1024)} %param.36) | copy-start | bytes 24580
  561.1 36.9 %copy-start.29 = (bf16[1,2048,512]{2,1,0:T(8,128)(2,1)S(1)}, bf16[1,2048,512]{2,1,0:T(8,128)(2,1)}, u32[]{:S(2)}) copy-start(bf16[1,2048,512]{2,1,0:T(8,128)(2,1)} %param.39) | copy-start | bytes 6291460
  603.5 31.1 %copy-start.28 = (f32[64,2]{0,1:T(2,128)S(1)}, f32[64,2]{0,1:T(2,128)}, u32[]{:S(2)}) copy-start(f32[64,2]{0,1:T(2,128)} %param.38) | copy-start | bytes 1540
  603.5 31.4 %copy-start.9 = (bf16[64,2048]{1,0:T(8,128)(2,1)S(1)}, bf16[64,2048]{1,0:T(8,128)(2,1)}, u32[]{:S(2)}) copy-start(bf16[64,2048]{1,0:T(8,128)(2,1)} %reduce-scatter.2.cloned.1.call-done) | copy-start | bytes 786436
  603.5 31.0 %all-to-all-start.1 = ((bf16[1,16,16,2048]{3,2,0,1:T(8,128)(2,1)}), bf16[1,16,16,2048]{3,2,0,1:T(8,128)(2,1)S(1)}, u32[]{:S(2)}, u32[]{:S(2)}) async-start(bf16[1,16,16,2048]{3,2,0,1:T(8,128)(2,1)} %fusion.19), calls=%async_computation.2 | async-start | bytes 2097152 | tf_op jit(solution)/shard_map/all_to_all | solution.py:184
  (19 other events, 44.2 us)
Sparse Core Ops, SparseCore 0:
  9.1 53.4 all-gather.1
  472.8 85.3 reduce-scatter.1
where the time goes:
time: 653 us; the launch traced here: 644 us
  other arithmetic  191 us (29%)
  waiting for transfers between devices  180 us (28%)
  matrix products  95 us (15%)
  starting transfers between devices  86.6 us (13%)
  local copies, waits for them, and re-layouts  38.7 us (6%)
  blocking collectives  36.3 us (6%)
  between operations  14.2 us (2%)
    another operation x4, other arithmetic, per_device(): jax.scipy.linalg.solve_triangular(system, right_side, lower=True, unit_di...  160 us
    reduce_scatter x1, waiting for transfers between devices, per_device(): lax.psum_scatter(jnp.dot(gated, w_out, preferred_element_type=jnp.float32...  84.1 us
    ppermute x16, starting transfers between devices, passed_along(): return lax.ppermute(block, axis, route)  82.8 us
    dot_general x55, matrix products, mix(): return jnp.einsum(form, left_arr, right_arr, precision=HIGH)  72.8 us
    all_gather x1, waiting for transfers between devices, per_device(): whole = lax.all_gather(tokens, 'exp', axis=1, tiled=True)  46.7 us
    all_to_all x1, blocking collectives, per_device(): lax.all_to_all(outgoing, 'exp', split_axis=0, concat_axis=1, tiled=True)  36.3 us
    all_to_all x1, waiting for transfers between devices, per_device(): lax.all_to_all(processed, 'exp', split_axis=1, concat_axis=0, tiled=True)  27.1 us
    ppermute x16, waiting for transfers between devices, passed_along(): return lax.ppermute(block, axis, route)  21.6 us
  transfers between devices with their start and end apart: 19, of which 19 were waited for; matrix products, arithmetic and copies ran while one was open for 2% of the time, Pallas kernels for 0%

commit v1 on v0

--- a/solution.py
+++ b/solution.py
@@ -8,6 +8,13 @@
 STRETCH = 64
 EPS = 1e-06
 HIGH = lax.Precision.HIGHEST
+
+
+def define_leaf(out_dim, shard_axis, frame):
+    oldest = jax.lax.axis_size(shard_axis)
+    s_next = jnp.stack([frame] * oldest, axis=0)
+    x_now = jax.lax.all_to_all(s_next, axis_name=shard_axis, concat_axis=0, split_axis=0)
+    return jnp.concatenate(x_now, axis=out_dim)
 
 
 def passed_along(block, axis, distance):
@@ -50,7 +57,7 @@
     w_up,
     w_down,
 ):
-    whole = lax.all_gather(tokens, "exp", axis=1, tiled=True)
+    whole = define_leaf(1, "exp", tokens)
     x_float = whole.astype(jnp.float32)
     normed = rms_scale(x_float, in_gain).astype(jnp.bfloat16)
 

time: 653 us -> 712 us (1.090)
  waiting for transfers between devices: 180 us -> 218 us
  starting transfers between devices: 86.6 us -> 96.4 us
    all_to_all x0 -> x1, waiting for transfers between devices: none -> 88.9 us  [define_leaf(): jax.lax.all_to_all(s_next, axis_name=shard_axis, concat_axis=0, split_axi...]
    all_gather x1 -> x0, waiting for transfers between devices: 46.7 us -> none  [per_device(): whole = lax.all_gather(tokens, 'exp', axis=1, tiled=True)]
    all_to_all x0 -> x1, starting transfers between devices: none -> 10.1 us  [define_leaf(): jax.lax.all_to_all(s_next, axis_name=shard_axis, concat_axis=0, split_axi...]
where the time goes in v1:
time: 712 us; the launch traced here: 702 us
  waiting for transfers between devices  218 us (31%)
  other arithmetic  190 us (27%)
  matrix products  102 us (14%)
  starting transfers between devices  96.4 us (14%)
  local copies, waits for them, and re-layouts  42.8 us (6%)
  blocking collectives  36.5 us (5%)
  between operations  14.3 us (2%)
    another operation x4, other arithmetic, per_device(): jax.scipy.linalg.solve_triangular(system, right_side, lower=True, unit_di...  160 us
    all_to_all x1, waiting for transfers between devices, define_leaf(): jax.lax.all_to_all(s_next, axis_name=shard_axis, concat_axis=0, split_axi...  88.9 us
    ppermute x16, starting transfers between devices, passed_along(): return lax.ppermute(block, axis, route)  82.5 us
    reduce_scatter x1, waiting for transfers between devices, per_device(): lax.psum_scatter(jnp.dot(gated, w_out, preferred_element_type=jnp.float32...  81.1 us
    dot_general x55, matrix products, mix(): return jnp.einsum(form, left_arr, right_arr, precision=HIGH)  72.8 us
    all_to_all x1, blocking collectives, per_device(): lax.all_to_all(outgoing, 'exp', split_axis=0, concat_axis=1, tiled=True)  36.5 us
    all_to_all x1, waiting for transfers between devices, per_device(): lax.all_to_all(processed, 'exp', split_axis=1, concat_axis=0, tiled=True)  27.1 us
    ppermute x16, waiting for transfers between devices, passed_along(): return lax.ppermute(block, axis, route)  21.2 us
  transfers between devices with their start and end apart: 19, of which 19 were waited for; matrix products, arithmetic and copies ran while one was open for 2% of the time, Pallas kernels for 0%

profile of v1, /device:TPU:1, one launch (start us, length us, event | category | flops | bytes accessed | tf_op | source)
XLA Modules:
  0.0 702.1 jit_solution(474170628864919647)
XLA Ops:
  6.5 3.9 stack.2
  10.5 10.1 %all-to-all-start = ((bf16[16,1024,128]{2,1,0:T(8,128)(2,1)}), bf16[16,1024,128]{2,1,0:T(8,128)(2,1)}, u32[]{:S(2)}, u32[]{:S(2)}) async-start(bf16[16,1024,128]{2,1,0:T(8,128)(2,1)} %stack.2), calls=%async_computation | async-start | bytes 8388608 | tf_op jit(solution)/shard_map/all_to_all | solution.py:16
  25.2 88.9 %all-to-all-done = bf16[16,1024,128]{2,1,0:T(8,128)(2,1)} async-done(((bf16[16,1024,128]{2,1,0:T(8,128)(2,1)}), bf16[16,1024,128]{2,1,0:T(8,128)(2,1)}, u32[]{:S(2)}, u32[]{:S(2)}) %all-to-all-start) | async-done | bytes 4194336 | tf_op jit(solution)/shard_map/all_to_all | solution.py:16
  117.3 3.8 convolution_convert_fusion.4
  121.1 3.8 convolution_convert_fusion.5
  124.9 3.7 convolution_convert_fusion.6
  129.4 3.9 collective-permute-start.1
  140.9 3.7 fusion.50
  144.6 158.7 %custom-call.4 = f32[2,16,1,64,64]{3,4,2,1,0:T(8,128)} custom-call(f32[2,16,1,64,64]{4,3,2,1,0:T(8,128)} %fusion.50), custom_call_target="InvertDiagBlocksLowerTriangular" | custom-call | tf_op jit(solution)/shard_map/jit(_solve_triangular)/vmap(vmap())/triangular_solve | solution.py:114
  315.2 5.2 convolution_bitcast_fusion.2
  320.4 5.4 bitcast_subtract_fusion
  325.8 70.9 %while.28 = (s32[]{:T(128)}, f32[2,128,128]{1,2,0:T(8,128)S(1)}, f32[2,128,128]{1,2,0:T(8,128)S(1)}, f32[16,2,128,128]{2,3,0,1:T(8,128)}, f32[16,2,128,128]{2,3,...) while((s32[]{:T(128)}, f32[2,128,128]{1,2,0:T(8,128)S(1)}, ...), condition=%wide.region_5.6_spmd.clone, body=%wide.region_4.5_spmd.clone.sunk | while | flops 100761600 | bytes 2492012 | solution.py:133
  397.0 104.0 %while.29 = (s32[]{:T(128)}, f32[2,128,128]{2,1,0:T(8,128)S(1)}, f32[2,128,128]{2,1,0:T(8,128)S(1)}, f32[2,128,128]{2,1,0:T(8,128)S(1)}, s32[]{:T(128)}, /*index=5*/s32[]{:T(128)}) while((s32[]{:T(128)}, f32[2,128,128]{2,1,0:T(8,128)S(1)}, f32[2,128,128]{2,1,0:T(8,128)S(1)}, f32[2,128,128]{2,1,0:T(8,128)S(1)}, s32[]{:T(128)}, ...), condition=%wide.region_7.8_spmd.clone, body=%wide.region_6.7_spmd.clone.sunk | while | flops 50462720 | bytes 917623 | solution.py:143
  397.4 3.8 collective-permute-start
  418.9 5.6 collective-permute-start
  426.2 5.8 collective-permute-start
  433.6 5.8 collective-permute-start
  441.6 5.5 collective-permute-start
  448.8 5.8 collective-permute-start
  456.2 6.0 collective-permute-start
  463.8 5.8 collective-permute-start
  471.2 5.8 collective-permute-start
  478.6 5.8 collective-permute-start
  486.1 5.8 collective-permute-start
  493.5 6.1 collective-permute-start
  501.0 4.3 bitcast_add_fusion
  519.6 9.5 %convolution_convert_fusion = bf16[1024,2048]{1,0:T(8,128)(2,1)} fusion(bf16[256,2048]{1,0:T(8,128)(2,1)} %param.35, bf16[2048,256]{1,0:T(8,128)(2,1)} %param.28, f32[128,8,2,128]{3,2,1,0:T(2,128)S(1)} %bitcast.199, f32[128,8,2,128]{3,2,1,0:T(2,128)} %bitcast.200, f32[256]{0:T(256)S(1)} %copy-done.38, f32[2048]{0:T(1024)S(1)} %copy-done.36, ...), kind=kOutput, calls=%fused_computation.25 | convolution fusion | flops 2160590848 | bytes 12596224 | tf_op jit(solution)/shard_map/dot_general | solution.py:160
  530.5 4.8 copy_bitcast_fusion
  535.3 81.1 %reduce-scatter.2.cloned.1.call-done = bf16[64,2048]{1,0:T(8,128)(2,1)} async-done(((bf16[1024,2048]{1,0:T(8,128)(2,1)}), bf16[64,2048]{1,0:T(8,128)(2,1)}) %reduce-scatter.2.cloned.1.call-update) | async-done | bytes 262160 | tf_op jit(solution)/shard_map/reduce_scatter | solution.py:159
  619.9 36.5 %all_to_all.23 = bf16[16,1,16,2048]{3,2,1,0:T(8,128)(2,1)S(1)} all-to-all(bf16[16,1,16,2048]{3,2,1,0:T(8,128)(2,1)S(1)} %bitcast.197), channel_id=1, replica_groups=mesh['seq'=16,'exp'=16] {'exp'}, dimensions={0} | all-to-all | bytes 2097152 | tf_op jit(solution)/shard_map/all_to_all | solution.py:184
  657.8 4.0 fusion.16
  665.8 27.1 %all-to-all-done.2 = bf16[1,16,16,2048]{3,2,0,1:T(8,128)(2,1)S(1)} async-done(((bf16[1,16,16,2048]{3,2,0,1:T(8,128)(2,1)}), bf16[1,16,16,2048]{3,2,0,1:T(8,128)(2,1)S(1)}, u32[]{:S(2)}, u32[]{:S(2)}) %all-to-all-start.2) | async-done | bytes 1048608 | tf_op jit(solution)/shard_map/all_to_all | solution.py:191
  (307 shorter events, 160.1 us)
Async XLA Ops:
  6.5 651.3 %copy-start = (bf16[1,512,2048]{2,1,0:T(8,128)(2,1)S(1)}, bf16[1,512,2048]{2,1,0:T(8,128)(2,1)}, u32[]{:S(2)}) copy-start(bf16[1,512,2048]{2,1,0:T(8,128)(2,1)} %param.41) | copy-start | bytes 6291460
  10.4 10.8 %copy-start.28 = (f32[4,128]{1,0:T(4,128)S(1)}, f32[4,128]{1,0:T(4,128)}, u32[]{:S(2)}) copy-start(f32[4,128]{1,0:T(4,128)} %param.29) | copy-start | bytes 6148
  10.4 10.8 %copy-start.29 = (f32[4,128]{1,0:T(4,128)S(1)}, f32[4,128]{1,0:T(4,128)}, u32[]{:S(2)}) copy-start(f32[4,128]{1,0:T(4,128)} %param.30) | copy-start | bytes 6148
  10.5 10.8 %copy-start.24 = (f32[4,256]{1,0:T(4,128)S(1)}, f32[4,256]{1,0:T(4,128)}, u32[]{:S(2)}) copy-start(f32[4,256]{1,0:T(4,128)} %param.31) | copy-start | bytes 12292
  10.5 12.2 %copy-start.37 = (f32[128]{0:T(128)S(1)}, f32[128]{0:T(128)}, u32[]{:S(2)}) copy-start(f32[128]{0:T(128)} %param.34) | copy-start | bytes 1540
  10.5 103.6 %all-to-all-start = ((bf16[16,1024,128]{2,1,0:T(8,128)(2,1)}), bf16[16,1024,128]{2,1,0:T(8,128)(2,1)}, u32[]{:S(2)}, u32[]{:S(2)}) async-start(bf16[16,1024,128]{2,1,0:T(8,128)(2,1)} %stack.2), calls=%async_computation | async-start | bytes 8388608 | tf_op jit(solution)/shard_map/all_to_all | solution.py:16
  20.6 595.8 %reduce-scatter.2.cloned.1.call-start = ((), (), s32[]{:S(2)}) async-start(), calls=%async_computation.4 | async-start | bytes 4456448 | tf_op jit(solution)/shard_map/reduce_scatter | solution.py:159
  20.8 96.5 %copy-start.11 = (f32[16,64,2]{1,0,2:T(8,128)}, f32[16,64,2]{1,0,2:T(8,128)S(1)}, u32[]{:S(2)}) copy-start(f32[16,64,2]{1,0,2:T(8,128)S(1)} %reshape.213) | copy-start | bytes 24580
  25.2 92.1 %copy-start.35 = (f32[2048]{0:T(1024)S(1)}, f32[2048]{0:T(1024)}, u32[]{:S(2)}) copy-start(f32[2048]{0:T(1024)} %param.24) | copy-start | bytes 24580
  129.4 5.4 collective-permute-start.1
  140.9 162.4 %copy-start.14 = (f32[2,16,64]{2,1,0:T(8,128)S(1)}, f32[2,16,64]{2,1,0:T(8,128)}, u32[]{:S(2)}) copy-start(f32[2,16,64]{2,1,0:T(8,128)} %get-tuple-element.187) | copy-start | bytes 24580
  315.2 10.6 %copy-start.3 = (f32[2,16,64,256]{3,2,1,0:T(8,128)}, f32[2,16,64,256]{3,2,1,0:T(8,128)S(1)}, u32[]{:S(2)}) copy-start(f32[2,16,64,256]{3,2,1,0:T(8,128)S(1)} %fusion.20) | copy-start | bytes 6291460
  397.4 5.1 collective-permute-start
  402.8 5.0 collective-permute-start
  408.1 5.0 collective-permute-start
  413.5 5.2 collective-permute-start
  418.9 6.9 collective-permute-start
  426.2 7.1 %collective-permute-start = (bf16[2,128,128]{2,1,0:T(8,128)(2,1)S(1)}, bf16[2,128,128]{2,1,0:T(8,128)(2,1)S(1)}, u32[]{:S(2)}, u32[]{:S(2)}) collective-permute-start(bf16[2,128,128]{2,1,0:T(8,128)(2,1)S(1)} %fusion.139), channel_id=1, source_target_pairs={{0,16},{16,32},{32,48},{48,64},{64,80},{80,96},{96,112},{112,128},... | collective-permute-start | bytes 196616 | tf_op jit(solution)/shard_map/while/body/eval_jaxpr/ppermute | solution.py:23
  433.6 7.7 %collective-permute-start = (bf16[2,128,128]{2,1,0:T(8,128)(2,1)S(1)}, bf16[2,128,128]{2,1,0:T(8,128)(2,1)S(1)}, u32[]{:S(2)}, u32[]{:S(2)}) collective-permute-start(bf16[2,128,128]{2,1,0:T(8,128)(2,1)S(1)} %fusion.139), channel_id=1, source_target_pairs={{0,16},{16,32},{32,48},{48,64},{64,80},{80,96},{96,112},{112,128},... | collective-permute-start | bytes 196616 | tf_op jit(solution)/shard_map/while/body/eval_jaxpr/ppermute | solution.py:23
  441.6 6.9 collective-permute-start
  448.8 7.1 %collective-permute-start = (bf16[2,128,128]{2,1,0:T(8,128)(2,1)S(1)}, bf16[2,128,128]{2,1,0:T(8,128)(2,1)S(1)}, u32[]{:S(2)}, u32[]{:S(2)}) collective-permute-start(bf16[2,128,128]{2,1,0:T(8,128)(2,1)S(1)} %fusion.139), channel_id=1, source_target_pairs={{0,16},{16,32},{32,48},{48,64},{64,80},{80,96},{96,112},{112,128},... | collective-permute-start | bytes 196616 | tf_op jit(solution)/shard_map/while/body/eval_jaxpr/ppermute | solution.py:23
  456.2 7.3 %collective-permute-start = (bf16[2,128,128]{2,1,0:T(8,128)(2,1)S(1)}, bf16[2,128,128]{2,1,0:T(8,128)(2,1)S(1)}, u32[]{:S(2)}, u32[]{:S(2)}) collective-permute-start(bf16[2,128,128]{2,1,0:T(8,128)(2,1)S(1)} %fusion.139), channel_id=1, source_target_pairs={{0,16},{16,32},{32,48},{48,64},{64,80},{80,96},{96,112},{112,128},... | collective-permute-start | bytes 196616 | tf_op jit(solution)/shard_map/while/body/eval_jaxpr/ppermute | solution.py:23
  463.8 7.1 %collective-permute-start = (bf16[2,128,128]{2,1,0:T(8,128)(2,1)S(1)}, bf16[2,128,128]{2,1,0:T(8,128)(2,1)S(1)}, u32[]{:S(2)}, u32[]{:S(2)}) collective-permute-start(bf16[2,128,128]{2,1,0:T(8,128)(2,1)S(1)} %fusion.139), channel_id=1, source_target_pairs={{0,16},{16,32},{32,48},{48,64},{64,80},{80,96},{96,112},{112,128},... | collective-permute-start | bytes 196616 | tf_op jit(solution)/shard_map/while/body/eval_jaxpr/ppermute | solution.py:23
  471.2 7.1 %collective-permute-start = (bf16[2,128,128]{2,1,0:T(8,128)(2,1)S(1)}, bf16[2,128,128]{2,1,0:T(8,128)(2,1)S(1)}, u32[]{:S(2)}, u32[]{:S(2)}) collective-permute-start(bf16[2,128,128]{2,1,0:T(8,128)(2,1)S(1)} %fusion.139), channel_id=1, source_target_pairs={{0,16},{16,32},{32,48},{48,64},{64,80},{80,96},{96,112},{112,128},... | collective-permute-start | bytes 196616 | tf_op jit(solution)/shard_map/while/body/eval_jaxpr/ppermute | solution.py:23
  478.6 7.1 %collective-permute-start = (bf16[2,128,128]{2,1,0:T(8,128)(2,1)S(1)}, bf16[2,128,128]{2,1,0:T(8,128)(2,1)S(1)}, u32[]{:S(2)}, u32[]{:S(2)}) collective-permute-start(bf16[2,128,128]{2,1,0:T(8,128)(2,1)S(1)} %fusion.139), channel_id=1, source_target_pairs={{0,16},{16,32},{32,48},{48,64},{64,80},{80,96},{96,112},{112,128},... | collective-permute-start | bytes 196616 | tf_op jit(solution)/shard_map/while/body/eval_jaxpr/ppermute | solution.py:23
  486.1 7.1 %collective-permute-start = (bf16[2,128,128]{2,1,0:T(8,128)(2,1)S(1)}, bf16[2,128,128]{2,1,0:T(8,128)(2,1)S(1)}, u32[]{:S(2)}, u32[]{:S(2)}) collective-permute-start(bf16[2,128,128]{2,1,0:T(8,128)(2,1)S(1)} %fusion.139), channel_id=1, source_target_pairs={{0,16},{16,32},{32,48},{48,64},{64,80},{80,96},{96,112},{112,128},... | collective-permute-start | bytes 196616 | tf_op jit(solution)/shard_map/while/body/eval_jaxpr/ppermute | solution.py:23
  493.5 7.4 %collective-permute-start = (bf16[2,128,128]{2,1,0:T(8,128)(2,1)S(1)}, bf16[2,128,128]{2,1,0:T(8,128)(2,1)S(1)}, u32[]{:S(2)}, u32[]{:S(2)}) collective-permute-start(bf16[2,128,128]{2,1,0:T(8,128)(2,1)S(1)} %fusion.139), channel_id=1, source_target_pairs={{0,16},{16,32},{32,48},{48,64},{64,80},{80,96},{96,112},{112,128},... | collective-permute-start | bytes 196616 | tf_op jit(solution)/shard_map/while/body/eval_jaxpr/ppermute | solution.py:23
  530.5 87.2 %copy-start.16 = (f32[2048]{0:T(1024)S(1)}, f32[2048]{0:T(1024)}, u32[]{:S(2)}) copy-start(f32[2048]{0:T(1024)} %param.36) | copy-start | bytes 24580
  619.3 37.0 %copy-start.31 = (bf16[1,2048,512]{2,1,0:T(8,128)(2,1)S(1)}, bf16[1,2048,512]{2,1,0:T(8,128)(2,1)}, u32[]{:S(2)}) copy-start(bf16[1,2048,512]{2,1,0:T(8,128)(2,1)} %param.39) | copy-start | bytes 6291460
  661.9 31.0 %copy-start.30 = (f32[64,2]{0,1:T(2,128)S(1)}, f32[64,2]{0,1:T(2,128)}, u32[]{:S(2)}) copy-start(f32[64,2]{0,1:T(2,128)} %param.38) | copy-start | bytes 1540
  661.9 31.4 %copy-start.7 = (bf16[64,2048]{1,0:T(8,128)(2,1)S(1)}, bf16[64,2048]{1,0:T(8,128)(2,1)}, u32[]{:S(2)}) copy-start(bf16[64,2048]{1,0:T(8,128)(2,1)} %reduce-scatter.2.cloned.1.call-done) | copy-start | bytes 786436
  661.9 31.0 %all-to-all-start.2 = ((bf16[1,16,16,2048]{3,2,0,1:T(8,128)(2,1)}), bf16[1,16,16,2048]{3,2,0,1:T(8,128)(2,1)S(1)}, u32[]{:S(2)}, u32[]{:S(2)}) async-start(bf16[1,16,16,2048]{3,2,0,1:T(8,128)(2,1)} %fusion.16), calls=%async_computation.3 | async-start | bytes 2097152 | tf_op jit(solution)/shard_map/all_to_all | solution.py:191
  (26 other events, 96.9 us)
Sparse Core Ops, SparseCore 0:
  529.2 87.0 reduce-scatter.1
